TPU v7x, 256 devices: a whole 4x4x8 slice. The times are simulated.
256 devices in a mesh: ctx: 128 (over y, x, z), head: 2 (over core).
Axes of the slice: x: 4, y: 4, z: 8, core: 2. Of those that a mesh axis runs over, the one named last changes fastest.
Arguments:
- queries: bfloat16 [16384, 4096], P('ctx', 'head'), may hold values from -9 to 9
- key_rows: bfloat16 [16384, 4096], P('ctx', 'head'), may hold values from -9 to 9
- value_rows: bfloat16 [16384, 4096], P('ctx', 'head'), may hold values from -6 to 6
- offsets: int32 [3, 32], P(None, 'head'), may hold values from 0 to 3, as said below
- sublayer_norm_gain: float32 [4096], P('head'), may hold values from 0.25 to 1.75
- cotangent: bfloat16 [16384, 4096], P('ctx', 'head'), may hold values from -6 to 6
Outputs:
- normed: bfloat16 [16384, 4096], P('ctx', 'head')
- query_grad: bfloat16 [16384, 4096], P('ctx', 'head')
- key_grad: bfloat16 [16384, 4096], P('ctx', 'head')
- value_grad: bfloat16 [16384, 4096], P('ctx', 'head')
Inputs may be any that keep to these rules, and one draw needn't show every extreme that they name: Row l holds offsets of 0 to 2**l - 1, and each of these values belongs to exactly 32 / 2**l heads.
All inputs are finite; a program needn't handle non-finite values.
Results may differ from a plain program's by a relative error of at most 0.007.
Values may be sent and summed in bfloat16 or wider, within the bound.
No kernel may reach another device: no remote copies, remote signals or barrier semaphores. Data moves between devices by JAX's collectives and lax.ppermute only.
A program may use at most 192 MiB of HBM per device.

v0:
```python
from functools import partial, reduce
import math
import jax
import jax.numpy as jnp
from jax import lax
from jax.sharding import PartitionSpec as P

SEG0 = 512
NEG_FILL = -1e30
EPSILON = 1e-05


def pick_rows(source, mask_table, stride):
    count = source.shape[0] // stride
    shaped = source.reshape((count, stride) + source.shape[1:])
    chosen = mask_table.reshape((1, stride, mask_table.shape[1]) + (1,) * (source.ndim - 2))
    return jnp.sum(jnp.where(chosen, shaped, jnp.zeros((), source.dtype)), axis=1)


def put_rows(picked, mask_table, stride, filler):
    chosen = mask_table.reshape((1, stride, mask_table.shape[1]) + (1,) * (picked.ndim - 2))
    spread = jnp.where(chosen, picked[:, None], jnp.asarray(filler, picked.dtype))
    return spread.reshape((picked.shape[0] * stride,) + picked.shape[1:])


def gather_group(members, group_axes):
    if not group_axes:
        return members
    return tuple((lax.all_gather(part, group_axes, axis=0, tiled=True) for part in members))


def grad_block(
    query_seg, key_seg, value_seg, dout_seg, lse_seg, delta_seg, score_scale, want_query, want_keys
):
    lse_t = jnp.transpose(lse_seg, (0, 2, 1))[..., None]
    delta_t = jnp.transpose(delta_seg, (0, 2, 1))[..., None]
    scores = (
        jnp.einsum("sqhd,skhd->shqk", query_seg, key_seg, preferred_element_type=jnp.float32)
        * score_scale
    )
    probs = jnp.exp(scores - lse_t)
    dprobs = jnp.einsum("sqhd,skhd->shqk", dout_seg, value_seg, preferred_element_type=jnp.float32)
    dscores = (probs * (dprobs - delta_t)).astype(jnp.bfloat16)
    query_part = None
    key_part = None
    value_part = None
    if want_query:
        query_part = (
            jnp.einsum("shqk,skhd->sqhd", dscores, key_seg, preferred_element_type=jnp.float32)
            * score_scale
        )
    if want_keys:
        probs_half = probs.astype(jnp.bfloat16)
        key_part = (
            jnp.einsum("shqk,sqhd->skhd", dscores, query_seg, preferred_element_type=jnp.float32)
            * score_scale
        )
        value_part = jnp.einsum(
            "shqk,sqhd->skhd", probs_half, dout_seg, preferred_element_type=jnp.float32
        )
    return (query_part, key_part, value_part)


def on_device(queries, key_rows, value_rows, offsets, sublayer_norm_gain, cotangent, level_axes):
    tok_rows = queries.shape[0]
    head_local = offsets.shape[1]
    head_size = queries.shape[1] // head_local
    level_count = offsets.shape[0]
    feature_total_count = lax.axis_size("head") * queries.shape[1]
    score_scale = 1.0 / math.sqrt(head_size)
    shape3 = (tok_rows, head_local, head_size)
    query_all = queries.reshape(shape3)
    key_all = key_rows.reshape(shape3)
    value_all = value_rows.reshape(shape3)

    def level_layout(level_num):
        stride = 2**level_num
        picked_rows = tok_rows // stride
        group_bits = level_axes[level_num]
        seg_count = max(1, picked_rows // SEG0)
        mask_table = jnp.arange(stride, dtype=jnp.int32)[:, None] == offsets[level_num][None, :]
        return (stride, picked_rows, group_bits, seg_count, mask_table)

    stored = []
    maxima = []
    totals = []
    partials = []
    for level_num in range(level_count):
        stride, picked_rows, group_bits, seg_count, mask_table = level_layout(level_num)
        query_sel = pick_rows(query_all, mask_table, stride)
        key_sel = pick_rows(key_all, mask_table, stride)
        value_sel = pick_rows(value_all, mask_table, stride)
        key_group, value_group = gather_group((key_sel, value_sel), group_bits)
        stored.append((key_group, value_group))
        query_seg = query_sel.reshape(seg_count, -1, head_local, head_size)
        key_seg = key_group.reshape(seg_count, SEG0, head_local, head_size)
        value_seg = value_group.reshape(seg_count, SEG0, head_local, head_size)
        scores = (
            jnp.einsum("sqhd,skhd->shqk", query_seg, key_seg, preferred_element_type=jnp.float32)
            * score_scale
        )
        row_max = jnp.max(scores, axis=-1)
        weights = jnp.exp(scores - row_max[..., None])
        row_total = jnp.sum(weights, axis=-1)
        level_out = jnp.einsum(
            "shqk,skhd->sqhd",
            weights.astype(jnp.bfloat16),
            value_seg,
            preferred_element_type=jnp.float32,
        )
        flat_max = jnp.transpose(row_max, (0, 2, 1)).reshape(picked_rows, head_local)
        flat_total = jnp.transpose(row_total, (0, 2, 1)).reshape(picked_rows, head_local)
        maxima.append(put_rows(flat_max, mask_table, stride, NEG_FILL))
        totals.append(put_rows(flat_total, mask_table, stride, 0.0))
        partials.append(
            put_rows(level_out.reshape(picked_rows, head_local, head_size), mask_table, stride, 0.0)
        )
    top_max = reduce(jnp.maximum, maxima)
    factors = [jnp.exp(each_max - top_max) for each_max in maxima]
    total = factors[0] * totals[0]
    summed = factors[0][..., None] * partials[0]
    for level_num in range(1, level_count):
        total = total + factors[level_num] * totals[level_num]
        summed = summed + factors[level_num][..., None] * partials[level_num]
    attended = (summed / total[..., None]).astype(jnp.bfloat16)
    log_total = top_max + jnp.log(total)
    attended_rows_flattened = attended.reshape(tok_rows, -1).astype(jnp.float32)
    first_sum, second_sum = lax.psum(
        (
            jnp.sum(attended_rows_flattened, axis=1),
            jnp.sum(attended_rows_flattened * attended_rows_flattened, axis=1),
        ),
        "head",
    )
    feature_mean = first_sum / feature_total_count
    variance = second_sum / feature_total_count - feature_mean * feature_mean
    inverse_deviation = 1.0 / jnp.sqrt(variance + EPSILON)
    normalized_input = (attended_rows_flattened - feature_mean[:, None]) * inverse_deviation[
        :, None
    ]
    normed = (normalized_input * sublayer_norm_gain[None, :]).astype(jnp.bfloat16)
    normalized_gradient = cotangent.astype(jnp.float32) * sublayer_norm_gain[None, :]
    gradient_sum_first, gradient_sum_second = lax.psum(
        (
            jnp.sum(normalized_gradient, axis=1),
            jnp.sum(normalized_gradient * normalized_input, axis=1),
        ),
        "head",
    )
    attended_gradient = (
        (
            normalized_gradient
            - gradient_sum_first[:, None] / feature_total_count
            - normalized_input * gradient_sum_second[:, None] / feature_total_count
        )
        * inverse_deviation[:, None]
    ).astype(jnp.bfloat16)
    dout_all = attended_gradient.reshape(shape3)
    delta = jnp.sum(dout_all.astype(jnp.float32) * attended.astype(jnp.float32), axis=-1)
    query_acc = jnp.zeros(shape3, jnp.float32)
    key_acc = jnp.zeros(shape3, jnp.float32)
    value_acc = jnp.zeros(shape3, jnp.float32)
    for level_num in range(level_count):
        stride, picked_rows, group_bits, seg_count, mask_table = level_layout(level_num)
        query_sel = pick_rows(query_all, mask_table, stride)
        key_sel = pick_rows(key_all, mask_table, stride)
        value_sel = pick_rows(value_all, mask_table, stride)
        dout_sel = pick_rows(dout_all, mask_table, stride)
        lse_sel = pick_rows(log_total, mask_table, stride)
        delta_sel = pick_rows(delta, mask_table, stride)
        key_group, value_group = stored[level_num]
        query_seg = query_sel.reshape(seg_count, -1, head_local, head_size)
        dout_seg = dout_sel.reshape(seg_count, -1, head_local, head_size)
        lse_seg = lse_sel.reshape(seg_count, -1, head_local)
        delta_seg = delta_sel.reshape(seg_count, -1, head_local)
        key_seg = key_group.reshape(seg_count, SEG0, head_local, head_size)
        value_seg = value_group.reshape(seg_count, SEG0, head_local, head_size)
        query_part, unused_key, unused_value = grad_block(
            query_seg, key_seg, value_seg, dout_seg, lse_seg, delta_seg, score_scale, True, False
        )
        query_group, dout_group, lse_group, delta_group = gather_group(
            (query_sel, dout_sel, lse_sel, delta_sel), group_bits
        )
        unused_query, key_part, value_part = grad_block(
            query_group.reshape(seg_count, SEG0, head_local, head_size),
            key_sel.reshape(seg_count, -1, head_local, head_size),
            value_sel.reshape(seg_count, -1, head_local, head_size),
            dout_group.reshape(seg_count, SEG0, head_local, head_size),
            lse_group.reshape(seg_count, SEG0, head_local),
            delta_group.reshape(seg_count, SEG0, head_local),
            score_scale,
            False,
            True,
        )
        key_own = key_part.reshape(picked_rows, head_local, head_size)
        value_own = value_part.reshape(picked_rows, head_local, head_size)
        query_acc = query_acc + put_rows(
            query_part.reshape(picked_rows, head_local, head_size), mask_table, stride, 0.0
        )
        key_acc = key_acc + put_rows(key_own, mask_table, stride, 0.0)
        value_acc = value_acc + put_rows(value_own, mask_table, stride, 0.0)
    flat_shape = (tok_rows, head_local * head_size)
    query_grad = query_acc.astype(jnp.bfloat16).reshape(flat_shape)
    key_grad = key_acc.astype(jnp.bfloat16).reshape(flat_shape)
    value_grad = value_acc.astype(jnp.bfloat16).reshape(flat_shape)
    return (normed, query_grad, key_grad, value_grad)


def split_mesh(mesh, tok_rows, level_count):
    ctx_count = mesh.shape["ctx"]
    sizes = sorted({max(1, SEG0 * 2**level_num // tok_rows) for level_num in range(level_count)})
    factors = []
    done = 1
    for size in sizes:
        if size > done:
            factors.append(size // done)
            done = size
    factors.append(ctx_count // done)
    names = tuple((f"c{index}" for index in range(len(factors))))
    shape = tuple(reversed(factors)) + (mesh.shape["head"],)
    sub_mesh = jax.sharding.Mesh(mesh.devices.reshape(shape), tuple(reversed(names)) + ("head",))
    level_axes = []
    for level_num in range(level_count):
        size = max(1, SEG0 * 2**level_num // tok_rows)
        count = 0
        span = 1
        while span < size:
            span *= factors[count]
            count += 1
        level_axes.append(tuple(reversed(names[:count])))
    return (sub_mesh, tuple(reversed(names)), level_axes)


def solution(mesh):

    def run(queries, key_rows, value_rows, offsets, sublayer_norm_gain, cotangent):
        tok_rows = queries.shape[0] // mesh.shape["ctx"]
        sub_mesh, ctx_axes, level_axes = split_mesh(mesh, tok_rows, offsets.shape[0])
        rows = P(ctx_axes, "head")
        in_specs = (rows, rows, rows, P(None, "head"), P("head"), rows)
        out_specs = (rows, rows, rows, rows)
        body = partial(on_device, level_axes=level_axes)
        return jax.shard_map(
            body, mesh=sub_mesh, in_specs=in_specs, out_specs=out_specs, check_vma=False
        )(queries, key_rows, value_rows, offsets, sublayer_norm_gain, cotangent)

    return run
```

profile of v0, /device:TPU:10, one launch (start us, length us, event | category | flops | bytes accessed | tf_op | source)
XLA Modules:
  0.0 700.7 jit_solution(9627745844129497146)
XLA Ops:
  24.4 40.6 %all-gather.17.cloned.1.call-done = bf16[512,16,128]{2,0,1:T(8,128)(2,1)} async-done(((bf16[128,16,128]{2,0,1:T(8,128)(2,1)}), bf16[512,16,128]{2,0,1:T(8,128)(2,1)}) %all-gather.17.cloned.1.call-update) | async-done | bytes 2097168 | tf_op jit(solution)/shard_map/all_gather | solution.py:29
  71.3 36.1 %all-gather.19.cloned.1.call-done = bf16[512,16,128]{2,0,1:T(8,128)(2,1)} async-done(((bf16[64,16,128]{2,0,1:T(8,128)(2,1)}), bf16[512,16,128]{2,0,1:T(8,128)(2,1)}) %all-gather.19.cloned.1.call-update) | async-done | bytes 2097168 | tf_op jit(solution)/shard_map/all_gather | solution.py:29
  112.6 36.0 %all-gather.25.cloned.1.call-done = bf16[512,16,128]{2,0,1:T(8,128)(2,1)} async-done(((bf16[64,16,128]{2,0,1:T(8,128)(2,1)}), bf16[512,16,128]{2,0,1:T(8,128)(2,1)}) %all-gather.25.cloned.1.call-update) | async-done | bytes 2097168 | tf_op jit(solution)/shard_map/all_gather | solution.py:29
  153.0 66.3 %all-gather.21.cloned.1.call-done = bf16[512,16,128]{2,0,1:T(8,128)(2,1)} async-done(((bf16[32,16,128]{2,0,1:T(8,128)(2,1)}), bf16[512,16,128]{2,0,1:T(8,128)(2,1)}) %all-gather.21.cloned.1.call-update) | async-done | bytes 2097168 | tf_op jit(solution)/shard_map/all_gather | solution.py:29
  219.2 2.6 fusion.116
  229.9 59.6 %all-gather.27.cloned.1.call-done = bf16[512,16,128]{2,0,1:T(8,128)(2,1)} async-done(((bf16[32,16,128]{2,0,1:T(8,128)(2,1)}), bf16[512,16,128]{2,0,1:T(8,128)(2,1)}) %all-gather.27.cloned.1.call-update) | async-done | bytes 2097168 | tf_op jit(solution)/shard_map/all_gather | solution.py:29
  293.2 2.5 copy.275
  297.2 42.7 %all-gather.23.cloned.1.call-done = bf16[512,16,128]{2,0,1:T(8,128)(2,1)} async-done(((bf16[128,16,128]{2,0,1:T(8,128)(2,1)}), bf16[512,16,128]{2,0,1:T(8,128)(2,1)}) %all-gather.23.cloned.1.call-update) | async-done | bytes 2097168 | tf_op jit(solution)/shard_map/all_gather | solution.py:29
  342.8 6.2 convert_reduce_fusion
  349.0 2.5 copy.263
  351.5 3.1 all-reduce.1
  355.3 3.8 fusion.66
  359.2 3.1 all-reduce
  363.0 2.7 multiply_convert_fusion.4
  385.0 6.9 all-gather.29.cloned.1.call-done
  391.9 4.4 fusion.117
  396.3 37.9 %all-gather.33.cloned.1.call-done = bf16[512,16,128]{2,0,1:T(8,128)(2,1)} async-done(((bf16[64,16,128]{2,0,1:T(8,128)(2,1)}), bf16[512,16,128]{2,0,1:T(8,128)(2,1)}) %all-gather.33.cloned.1.call-update) | async-done | bytes 2097168 | tf_op jit(solution)/shard_map/all_gather | solution.py:29
  434.2 3.8 fusion.111
  459.9 24.8 %all-gather.1 = f32[8,64,16]{1,2,0:T(8,128)S(1)} all-gather(f32[1,64,16]{1,2,0:T(8,128)} %copy.335), channel_id=1, replica_groups=mesh['c3'=8,'c2'=2,'c1'=2,'c0'=4,'head'=2] {'c1','c0'}, dimensions={0}, use_global_device_ids=true | all-gather | bytes 36864 | tf_op jit(solution)/shard_map/all_gather | solution.py:29
  486.9 24.7 %all-gather = f32[8,64,16]{1,2,0:T(8,128)S(1)} all-gather(f32[1,64,16]{1,2,0:T(8,128)} %copy.331), channel_id=1, replica_groups=mesh['c3'=8,'c2'=2,'c1'=2,'c0'=4,'head'=2] {'c1','c0'}, dimensions={0}, use_global_device_ids=true | all-gather | bytes 36864 | tf_op jit(solution)/shard_map/all_gather | solution.py:29
  526.4 32.3 %all-gather.2 = f32[16,32,16]{1,2,0:T(8,128)S(1)} all-gather(f32[1,32,16]{1,2,0:T(8,128)S(1)} %copy.341), channel_id=1, replica_groups=mesh['c3'=8,'c2'=2,'c1'=2,'c0'=4,'head'=2] {'c2','c1','c0'}, dimensions={0}, use_global_device_ids=true | all-gather | bytes 34816 | tf_op jit(solution)/shard_map/all_gather | solution.py:29
  561.0 31.9 %all-gather.3 = f32[16,32,16]{1,2,0:T(8,128)S(1)} all-gather(f32[1,32,16]{1,2,0:T(8,128)S(1)} %copy.345), channel_id=1, replica_groups=mesh['c3'=8,'c2'=2,'c1'=2,'c0'=4,'head'=2] {'c2','c1','c0'}, dimensions={0}, use_global_device_ids=true | all-gather | bytes 34816 | tf_op jit(solution)/shard_map/all_gather | solution.py:29
  597.8 4.1 fusion.33
  603.7 3.5 fusion.27
  611.0 14.2 %all_gather.61 = f32[512,16]{0,1:T(8,128)} all-gather(f32[128,16]{0,1:T(8,128)} %get-tuple-element.38), channel_id=1, replica_groups=mesh['c3'=8,'c2'=2,'c1'=2,'c0'=4,'head'=2] {'c0'}, dimensions={0}, use_global_device_ids=true | all-gather | bytes 40960 | tf_op jit(solution)/shard_map/all_gather | solution.py:29
  626.0 13.9 %all_gather.63 = f32[512,16]{0,1:T(8,128)} all-gather(f32[128,16]{0,1:T(8,128)S(1)} %broadcast_select_fusion.8), channel_id=1, replica_groups=mesh['c3'=8,'c2'=2,'c1'=2,'c0'=4,'head'=2] {'c0'}, dimensions={0}, use_global_device_ids=true | all-gather | bytes 40960 | tf_op jit(solution)/shard_map/all_gather | solution.py:29
  644.0 6.0 fusion.21
  649.9 5.9 fusion.3
  655.8 6.7 convolution_multiply_fusion.1
  665.8 4.2 fusion.25
  677.2 3.4 fusion.31
  685.4 4.2 fusion.50
  (268 shorter events, 144.9 us)
Async XLA Ops:
  7.2 57.9 %all-gather.17.cloned.1.call-start = ((), (), s32[]{:S(2)}) async-start(), calls=%async_computation | async-start | bytes 2621440 | tf_op jit(solution)/shard_map/all_gather | solution.py:29
  8.0 13.4 %copy-start.39 = (pred[16]{0:T(512)(128)(4,1)}, pred[16]{0:T(512)(128)(4,1)S(1)}, u32[]{:S(2)}) copy-start(pred[16]{0:T(512)(128)(4,1)S(1)} %compare_bitcast_fusion) | copy-start | bytes 52
  12.1 95.3 %all-gather.19.cloned.1.call-start = ((), (), s32[]{:S(2)}) async-start(), calls=%async_computation.1 | async-start | bytes 2359296 | tf_op jit(solution)/shard_map/all_gather | solution.py:29
  13.2 9.5 %copy-start.46 = (pred[2,16]{1,0:T(4,128)(4,1)}, pred[2,16]{1,0:T(4,128)(4,1)S(1)}, u32[]{:S(2)}) copy-start(pred[2,16]{1,0:T(4,128)(4,1)S(1)} %iota_compare_fusion.1) | copy-start | bytes 100
  13.9 4.0 copy-start.10
  14.7 133.9 %all-gather.25.cloned.1.call-start = ((), (), s32[]{:S(2)}) async-start(), calls=%async_computation.4 | async-start | bytes 2359296 | tf_op jit(solution)/shard_map/all_gather | solution.py:29
  15.6 203.6 %all-gather.21.cloned.1.call-start = ((), (), s32[]{:S(2)}) async-start(), calls=%async_computation.2 | async-start | bytes 2228224 | tf_op jit(solution)/shard_map/all_gather | solution.py:29
  15.7 6.3 copy-start.47
  15.7 7.7 %copy-start.21 = (bf16[128,2048]{1,0:T(8,128)(2,1)S(1)}, bf16[128,2048]{1,0:T(8,128)(2,1)}, u32[]{:S(2)}) copy-start(bf16[128,2048]{1,0:T(8,128)(2,1)} %param.11) | copy-start | bytes 1572868
  16.3 8.1 %copy-start.17 = (bf16[32,16,128]{2,1,0:T(8,128)(2,1)}, bf16[32,16,128]{2,1,0:T(8,128)(2,1)S(1)}, u32[]{:S(2)}) copy-start(bf16[32,16,128]{2,1,0:T(8,128)(2,1)S(1)} %get-tuple-element.32) | copy-start | bytes 393220
  16.3 8.1 %copy-start.18 = (bf16[32,16,128]{2,1,0:T(8,128)(2,1)}, bf16[32,16,128]{2,1,0:T(8,128)(2,1)S(1)}, u32[]{:S(2)}) copy-start(bf16[32,16,128]{2,1,0:T(8,128)(2,1)S(1)} %get-tuple-element.31) | copy-start | bytes 393220
  16.3 48.7 %copy-start.6 = (bf16[128,16,128]{2,0,1:T(8,128)(2,1)S(1)}, bf16[128,16,128]{2,0,1:T(8,128)(2,1)}, u32[]{:S(2)}) copy-start(bf16[128,16,128]{2,0,1:T(8,128)(2,1)} %get-tuple-element.62) | copy-start | bytes 1572868
  17.1 272.4 %all-gather.27.cloned.1.call-start = ((), (), s32[]{:S(2)}) async-start(), calls=%async_computation.5 | async-start | bytes 2228224 | tf_op jit(solution)/shard_map/all_gather | solution.py:29
  17.9 322.1 %all-gather.23.cloned.1.call-start = ((), (), s32[]{:S(2)}) async-start(), calls=%async_computation.3 | async-start | bytes 2621440 | tf_op jit(solution)/shard_map/all_gather | solution.py:29
  18.4 373.5 %all-gather.29.cloned.1.call-start = ((), (), s32[]{:S(2)}) async-start(), calls=%async_computation.6 | async-start | bytes 2621440 | tf_op jit(solution)/shard_map/all_gather | solution.py:29
  19.2 415.0 %all-gather.33.cloned.1.call-start = ((), (), s32[]{:S(2)}) async-start(), calls=%async_computation.8 | async-start | bytes 2359296 | tf_op jit(solution)/shard_map/all_gather | solution.py:29
  20.0 621.3 %all-gather.37.cloned.1.call-start = ((), (), s32[]{:S(2)}) async-start(), calls=%async_computation.10 | async-start | bytes 2228224 | tf_op jit(solution)/shard_map/all_gather | solution.py:29
  20.8 629.1 %all-gather.31.cloned.1.call-start = ((), (), s32[]{:S(2)}) async-start(), calls=%async_computation.7 | async-start | bytes 2621440 | tf_op jit(solution)/shard_map/all_gather | solution.py:29
  22.0 45.4 %copy-start.27 = (pred[32,4,16]{2,1,0:T(4,128)(4,1)}, pred[32,4,16]{2,1,0:T(4,128)(4,1)S(1)}, u32[]{:S(2)}) copy-start(pred[32,4,16]{2,1,0:T(4,128)(4,1)S(1)} %broadcast_in_dim.468) | copy-start | bytes 6148
  67.4 3.8 copy-start.24
  109.9 38.8 %copy-start.23 = (f32[16,64]{1,0:T(8,128)}, f32[16,64]{1,0:T(8,128)S(1)}, u32[]{:S(2)}) copy-start(f32[16,64]{1,0:T(8,128)S(1)} %get-tuple-element.65) | copy-start | bytes 12292
  355.3 3.8 copy-start.48
  355.3 3.8 copy-start.49
  369.7 292.8 %all-gather.35.cloned.1.call-start = ((), (), s32[]{:S(2)}) async-start(), calls=%async_computation.9 | async-start | bytes 2359296 | tf_op jit(solution)/shard_map/all_gather | solution.py:29
  376.2 298.7 %all-gather.39.cloned.1.call-start = ((), (), s32[]{:S(2)}) async-start(), calls=%async_computation.11 | async-start | bytes 2228224 | tf_op jit(solution)/shard_map/all_gather | solution.py:29
  434.2 3.8 copy-start.22
  597.7 6.0 copy-start.31
  597.8 6.0 copy-start.32
  609.4 30.6 %copy-start.26 = (f32[16,128]{1,0:T(8,128)S(1)}, f32[16,128]{1,0:T(8,128)}, u32[]{:S(2)}) copy-start(f32[16,128]{1,0:T(8,128)} %copy-done.24) | copy-start | bytes 24580
  609.4 30.5 %copy-start.29 = (f32[16,128]{1,0:T(8,128)S(1)}, f32[16,128]{1,0:T(8,128)}, u32[]{:S(2)}) copy-start(f32[16,128]{1,0:T(8,128)} %fusion) | copy-start | bytes 24580
  611.0 32.9 %copy-start.2 = (bf16[512,16,128]{2,0,1:T(8,128)(2,1)S(1)}, bf16[512,16,128]{2,0,1:T(8,128)(2,1)}, u32[]{:S(2)}) copy-start(bf16[512,16,128]{2,0,1:T(8,128)(2,1)} %all-gather.17.cloned.1.call-done) | copy-start | bytes 6291460
  655.8 6.7 copy-start.1
  (31 other events, 59.3 us)
Sparse Core Ops, SparseCore 0:
  12.2 52.8 all-gather.16
  66.8 40.4 all-gather.18
  109.1 39.4 all-gather.24
  150.3 68.9 all-gather.20
  220.9 68.5 all-gather.26
  291.7 48.1 all-gather.22
  342.3 49.5 all-gather.28
  393.7 40.4 all-gather.32
  436.0 68.9 all-gather.36
  506.6 49.5 all-gather.30
  558.0 40.7 all-gather.34
  600.5 68.6 all-gather.38
where the time goes:
time: 707 us; the launch traced here: 701 us
  waiting for transfers between devices  327 us (46%)
  blocking collectives  148 us (21%)
  local copies, waits for them, and re-layouts  109 us (15%)
  matrix products  66.7 us (9%)
  other arithmetic  33.2 us (5%)
  between operations  15.3 us (2%)
    all_gather x12, waiting for transfers between devices, gather_group(): lax.all_gather(part, group_axes, axis=0, tiled=True)  326 us
    all_gather x6, blocking collectives, gather_group(): lax.all_gather(part, group_axes, axis=0, tiled=True)  142 us
    broadcast_in_dim x45, local copies, waits for them, and re-layouts, put_rows(): jnp.where(chosen, picked[:, None], jnp.asarray(filler, picked.dtype))  36.9 us
    unnamed x128, local copies, waits for them, and re-layouts  24.1 us
    dot_general x3, matrix products, grad_block(): jnp.einsum('shqk,sqhd->skhd', dscores, query_seg, preferred_element_type=...  14.3 us
  transfers between devices with their start and end apart: 12, of which 8 were waited for; matrix products, arithmetic and copies ran while one was open for 26% of the time, Pallas kernels for 0%

commit v1 on v0

--- a/solution.py
+++ b/solution.py
@@ -26,7 +26,15 @@
 def gather_group(members, group_axes):
     if not group_axes:
         return members
-    return tuple((lax.all_gather(part, group_axes, axis=0, tiled=True) for part in members))
+    return tuple(
+        (
+            jnp.concatenate(
+                lax.all_to_all(jnp.stack([part] * lax.axis_size(group_axes)), group_axes, 0, 0),
+                axis=0,
+            )
+            for part in members
+        )
+    )
 
 
 def grad_block(

time: 707 us -> 839 us (1.19)
  waiting for transfers between devices: 327 us -> 417 us
  blocking collectives: 148 us -> 60.2 us
  starting transfers between devices: 1.13 us -> 84.3 us
  local copies, waits for them, and re-layouts: 109 us -> 169 us
  between operations: 15.3 us -> 2.11 us
  matrix products: 66.7 us -> 56.1 us
    all_to_all x0 -> x17, waiting for transfers between devices: none -> 417 us  [gather_group(): lax.all_to_all(jnp.stack([part] * lax.axis_size(group_axes)), group_axes,...]
    all_gather x12 -> x0, waiting for transfers between devices: 326 us -> none  [gather_group(): lax.all_gather(part, group_axes, axis=0, tiled=True)]
    all_gather x6 -> x0, blocking collectives: 142 us -> none  [gather_group(): lax.all_gather(part, group_axes, axis=0, tiled=True)]
    all_to_all x0 -> x17, starting transfers between devices: none -> 84.3 us  [gather_group(): lax.all_to_all(jnp.stack([part] * lax.axis_size(group_axes)), group_axes,...]
    all_to_all x0 -> x1, blocking collectives: none -> 54 us  [gather_group(): lax.all_to_all(jnp.stack([part] * lax.axis_size(group_axes)), group_axes,...]
    another operation x4 -> x20, local copies, waits for them, and re-layouts: 2.92 us -> 32.6 us  [the longest x14 28.5 us: gather_group(): jnp.stack([part] * lax.axis_size(group_axes))]
    all_to_all x0 -> x18, local copies, waits for them, and re-layouts: none -> 26.5 us  [gather_group(): lax.all_to_all(jnp.stack([part] * lax.axis_size(group_axes)), group_axes,...]
    mul x0 -> x6, local copies, waits for them, and re-layouts: none -> 13 us  [the longest x4 8.63 us: on_device(): summed = summed + factors[level_num][..., None] * partials[level_num]]
  transfers between devices with their start and end apart: 12 -> 17, of which waited for: 8 -> 15; matrix products, arithmetic and copies ran while one was open for 26% -> 25% of each run, Pallas kernels for 0% -> 0%
where the time goes in v1:
time: 839 us; the launch traced here: 828 us
  waiting for transfers between devices  417 us (50%)
  local copies, waits for them, and re-layouts  169 us (20%)
  starting transfers between devices  84.3 us (10%)
  blocking collectives  60.2 us (7%)
  matrix products  56.1 us (7%)
  other arithmetic  38.6 us (5%)
    all_to_all x17, waiting for transfers between devices, gather_group(): lax.all_to_all(jnp.stack([part] * lax.axis_size(group_axes)), group_axes,...  417 us
    all_to_all x17, starting transfers between devices, gather_group(): lax.all_to_all(jnp.stack([part] * lax.axis_size(group_axes)), group_axes,...  84.3 us
    all_to_all x1, blocking collectives, gather_group(): lax.all_to_all(jnp.stack([part] * lax.axis_size(group_axes)), group_axes,...  54 us
    broadcast_in_dim x39, local copies, waits for them, and re-layouts, put_rows(): jnp.where(chosen, picked[:, None], jnp.asarray(filler, picked.dtype))  29 us
    another operation x14, local copies, waits for them, and re-layouts, gather_group(): jnp.stack([part] * lax.axis_size(group_axes))  28.5 us
    unnamed x155, local copies, waits for them, and re-layouts  28 us
    all_to_all x18, local copies, waits for them, and re-layouts, gather_group(): lax.all_to_all(jnp.stack([part] * lax.axis_size(group_axes)), group_axes,...  26.5 us
  transfers between devices with their start and end apart: 17, of which 15 were waited for; matrix products, arithmetic and copies ran while one was open for 25% of the time, Pallas kernels for 0%

profile of v1, /device:TPU:10, one launch (start us, length us, event | category | flops | bytes accessed | tf_op | source)
XLA Modules:
  0.0 828.0 jit_solution(2458320936791799907)
XLA Ops:
  5.4 54.0 %all_to_all.90 = bf16[4,128,16,128]{3,1,2,0:T(8,128)(2,1)} all-to-all(bf16[4,128,16,128]{3,1,2,0:T(8,128)(2,1)S(1)} %stack.36), channel_id=1, replica_groups=mesh['c3'=8,'c2'=2,'c1'=2,'c0'=4,'head'=2] {'c0'}, dimensions={0} | all-to-all | bytes 4194304 | tf_op jit(solution)/shard_map/all_to_all | solution.py:32
  65.2 47.1 %all-to-all-done.3 = bf16[4,128,16,128]{1,3,2,0:T(8,128)(2,1)S(1)} async-done(((bf16[4,128,16,128]{1,3,2,0:T(8,128)(2,1)}), bf16[4,128,16,128]{1,3,2,0:T(8,128)(2,1)S(1)}, u32[]{:S(2)}, u32[]{:S(2)}) %all-to-all-start.3) | async-done | bytes 2097184 | tf_op jit(solution)/shard_map/all_to_all | solution.py:32
  123.2 42.3 %all-to-all-done.6 = bf16[4,128,16,128]{3,1,2,0:T(8,128)(2,1)S(1)} async-done(((bf16[4,128,16,128]{3,1,2,0:T(8,128)(2,1)}), bf16[4,128,16,128]{3,1,2,0:T(8,128)(2,1)S(1)}, u32[]{:S(2)}, u32[]{:S(2)}) %all-to-all-start.6) | async-done | bytes 2097184 | tf_op jit(solution)/shard_map/all_to_all | solution.py:32
  168.6 6.6 all-to-all-start.1
  175.2 50.6 %all-to-all-done.1 = bf16[8,64,16,128]{3,1,2,0:T(8,128)(2,1)} async-done(((bf16[8,64,16,128]{3,1,2,0:T(8,128)(2,1)}), bf16[8,64,16,128]{3,1,2,0:T(8,128)(2,1)}, u32[]{:S(2)}, u32[]{:S(2)}) %all-to-all-start.1) | async-done | bytes 2097184 | tf_op jit(solution)/shard_map/all_to_all | solution.py:32
  233.0 49.8 %all-to-all-done.4 = bf16[8,64,16,128]{3,1,2,0:T(8,128)(2,1)S(1)} async-done(((bf16[8,64,16,128]{3,1,2,0:T(8,128)(2,1)}), bf16[8,64,16,128]{3,1,2,0:T(8,128)(2,1)S(1)}, u32[]{:S(2)}, u32[]{:S(2)}) %all-to-all-start.4) | async-done | bytes 2097184 | tf_op jit(solution)/shard_map/all_to_all | solution.py:32
  292.5 46.4 %all-to-all-done.10 = bf16[8,64,16,128]{3,1,2,0:T(8,128)(2,1)S(1)} async-done(((bf16[8,64,16,128]{3,1,2,0:T(8,128)(2,1)}), bf16[8,64,16,128]{3,1,2,0:T(8,128)(2,1)S(1)}, u32[]{:S(2)}, u32[]{:S(2)}) %all-to-all-start.10) | async-done | bytes 2097184 | tf_op jit(solution)/shard_map/all_to_all | solution.py:32
  340.9 4.7 all-to-all-start.2
  345.7 47.6 %all-to-all-done.2 = bf16[16,32,16,128]{3,1,2,0:T(8,128)(2,1)} async-done(((bf16[16,32,16,128]{3,1,2,0:T(8,128)(2,1)}), bf16[16,32,16,128]{3,1,2,0:T(8,128)(2,1)}, u32[]{:S(2)}, u32[]{:S(2)}) %all-to-all-start.2) | async-done | bytes 2097184 | tf_op jit(solution)/shard_map/all_to_all | solution.py:32
  395.1 8.5 %all-to-all-start.5 = ((bf16[16,32,16,128]{3,1,2,0:T(8,128)(2,1)}), bf16[16,32,16,128]{3,1,2,0:T(8,128)(2,1)}, u32[]{:S(2)}, u32[]{:S(2)}) async-start(bf16[16,32,16,128]{3,1,2,0:T(8,128)(2,1)} %stack.41), calls=%async_computation.5 | async-start | bytes 4194304 | tf_op jit(solution)/shard_map/all_to_all | solution.py:32
  428.1 23.3 %all-to-all-done.5 = bf16[16,32,16,128]{3,1,2,0:T(8,128)(2,1)} async-done(((bf16[16,32,16,128]{3,1,2,0:T(8,128)(2,1)}), bf16[16,32,16,128]{3,1,2,0:T(8,128)(2,1)}, u32[]{:S(2)}, u32[]{:S(2)}) %all-to-all-start.5) | async-done | bytes 2097184 | tf_op jit(solution)/shard_map/all_to_all | solution.py:32
  454.1 7.5 all-to-all-start.14
  479.8 6.5 convert_reduce_fusion
  509.9 6.0 fusion.69
  548.8 4.5 all-to-all-start.7
  554.1 5.0 all-to-all-done.7
  569.3 6.0 all-to-all-start.11
  578.9 4.5 all-to-all-done.11
  590.4 4.9 all-to-all-done.13
  595.3 4.5 all-to-all-start.15
  602.1 5.0 all-to-all-done.15
  607.1 5.2 all-to-all-start.17
  614.2 5.4 all-to-all-done.17
  622.6 4.6 all-to-all-start.8
  630.9 38.0 %all-to-all-done.8 = bf16[4,128,16,128]{1,3,2,0:T(8,128)(2,1)} async-done(((bf16[4,128,16,128]{1,3,2,0:T(8,128)(2,1)}), bf16[4,128,16,128]{1,3,2,0:T(8,128)(2,1)}, u32[]{:S(2)}, u32[]{:S(2)}) %all-to-all-start.8) | async-done | bytes 2097184 | tf_op jit(solution)/shard_map/all_to_all | solution.py:32
  671.8 4.4 all-to-all-start.12
  681.0 44.6 %all-to-all-done.12 = bf16[8,64,16,128]{3,1,2,0:T(8,128)(2,1)} async-done(((bf16[8,64,16,128]{3,1,2,0:T(8,128)(2,1)}), bf16[8,64,16,128]{3,1,2,0:T(8,128)(2,1)}, u32[]{:S(2)}, u32[]{:S(2)}) %all-to-all-start.12) | async-done | bytes 2097184 | tf_op jit(solution)/shard_map/all_to_all | solution.py:32
  728.2 5.7 all-to-all-start.16
  733.9 4.5 fusion.119
  741.5 6.7 convolution_multiply_fusion.2
  782.3 6.3 convolution_multiply_fusion.1
  791.3 4.8 fusion.3
  (327 shorter events, 260.5 us)
Async XLA Ops:
  1.4 406.3 %copy-start.55 = (pred[16]{0:T(512)(128)(4,1)}, pred[16]{0:T(512)(128)(4,1)S(1)}, u32[]{:S(2)}) copy-start(pred[16]{0:T(512)(128)(4,1)S(1)} %compare_bitcast_fusion) | copy-start | bytes 52
  4.5 54.9 %copy-start.20 = (bf16[128,16,128]{0,2,1:T(8,128)(2,1)}, bf16[128,16,128]{0,2,1:T(8,128)(2,1)S(1)}, u32[]{:S(2)}) copy-start(bf16[128,16,128]{0,2,1:T(8,128)(2,1)S(1)} %get-tuple-element.44) | copy-start | bytes 1572868
  4.5 54.9 %copy-start.37 = (bf16[128,16,128]{0,2,1:T(8,128)(2,1)}, bf16[128,16,128]{0,2,1:T(8,128)(2,1)S(1)}, u32[]{:S(2)}) copy-start(bf16[128,16,128]{0,2,1:T(8,128)(2,1)S(1)} %get-tuple-element.43) | copy-start | bytes 1572868
  4.5 60.4 %copy-start.21 = (bf16[128,16,128]{0,2,1:T(8,128)(2,1)}, bf16[128,16,128]{0,2,1:T(8,128)(2,1)S(1)}, u32[]{:S(2)}) copy-start(bf16[128,16,128]{0,2,1:T(8,128)(2,1)S(1)} %get-tuple-element.45) | copy-start | bytes 1572868
  61.3 51.0 %all-to-all-start.3 = ((bf16[4,128,16,128]{1,3,2,0:T(8,128)(2,1)}), bf16[4,128,16,128]{1,3,2,0:T(8,128)(2,1)S(1)}, u32[]{:S(2)}, u32[]{:S(2)}) async-start(bf16[4,128,16,128]{1,3,2,0:T(8,128)(2,1)} %stack.39), calls=%async_computation.3 | async-start | bytes 4194304 | tf_op jit(solution)/shard_map/all_to_all | solution.py:32
  114.2 51.3 %all-to-all-start.6 = ((bf16[4,128,16,128]{3,1,2,0:T(8,128)(2,1)}), bf16[4,128,16,128]{3,1,2,0:T(8,128)(2,1)S(1)}, u32[]{:S(2)}, u32[]{:S(2)}) async-start(bf16[4,128,16,128]{3,1,2,0:T(8,128)(2,1)} %stack.42), calls=%async_computation.6 | async-start | bytes 4194304 | tf_op jit(solution)/shard_map/all_to_all | solution.py:32
  120.4 283.4 %copy-start.60 = (pred[2,16]{1,0:T(4,128)(4,1)}, pred[2,16]{1,0:T(4,128)(4,1)S(1)}, u32[]{:S(2)}) copy-start(pred[2,16]{1,0:T(4,128)(4,1)S(1)} %iota_compare_fusion.1) | copy-start | bytes 100
  168.6 57.2 %all-to-all-start.1 = ((bf16[8,64,16,128]{3,1,2,0:T(8,128)(2,1)}), bf16[8,64,16,128]{3,1,2,0:T(8,128)(2,1)}, u32[]{:S(2)}, u32[]{:S(2)}) async-start(bf16[8,64,16,128]{3,1,2,0:T(8,128)(2,1)} %stack.37), calls=%async_computation.1 | async-start | bytes 4194304 | tf_op jit(solution)/shard_map/all_to_all | solution.py:32
  227.6 55.1 %all-to-all-start.4 = ((bf16[8,64,16,128]{3,1,2,0:T(8,128)(2,1)}), bf16[8,64,16,128]{3,1,2,0:T(8,128)(2,1)S(1)}, u32[]{:S(2)}, u32[]{:S(2)}) async-start(bf16[8,64,16,128]{3,1,2,0:T(8,128)(2,1)} %stack.40), calls=%async_computation.4 | async-start | bytes 4194304 | tf_op jit(solution)/shard_map/all_to_all | solution.py:32
  285.8 53.1 %all-to-all-start.10 = ((bf16[8,64,16,128]{3,1,2,0:T(8,128)(2,1)}), bf16[8,64,16,128]{3,1,2,0:T(8,128)(2,1)S(1)}, u32[]{:S(2)}, u32[]{:S(2)}) async-start(bf16[8,64,16,128]{3,1,2,0:T(8,128)(2,1)} %stack.46), calls=%async_computation.10 | async-start | bytes 4194304 | tf_op jit(solution)/shard_map/all_to_all | solution.py:32
  289.4 114.2 %copy-start.62 = (pred[4,16]{1,0:T(4,128)(4,1)}, pred[4,16]{1,0:T(4,128)(4,1)S(1)}, u32[]{:S(2)}) copy-start(pred[4,16]{1,0:T(4,128)(4,1)S(1)} %iota_compare_fusion) | copy-start | bytes 196
  340.9 52.4 %all-to-all-start.2 = ((bf16[16,32,16,128]{3,1,2,0:T(8,128)(2,1)}), bf16[16,32,16,128]{3,1,2,0:T(8,128)(2,1)}, u32[]{:S(2)}, u32[]{:S(2)}) async-start(bf16[16,32,16,128]{3,1,2,0:T(8,128)(2,1)} %stack.38), calls=%async_computation.2 | async-start | bytes 4194304 | tf_op jit(solution)/shard_map/all_to_all | solution.py:32
  395.1 11.8 %copy-start.39 = (bf16[32,16,128]{2,1,0:T(8,128)(2,1)S(1)}, bf16[32,16,128]{2,1,0:T(8,128)(2,1)}, u32[]{:S(2)}) copy-start(bf16[32,16,128]{2,1,0:T(8,128)(2,1)} %get-tuple-element.17) | copy-start | bytes 393220
  395.1 13.2 %copy-start.14 = (bf16[4,128,16,128]{3,1,2,0:T(8,128)(2,1)S(1)}, bf16[4,128,16,128]{3,1,2,0:T(8,128)(2,1)}, u32[]{:S(2)}) copy-start(bf16[4,128,16,128]{3,1,2,0:T(8,128)(2,1)} %all_to_all.90) | copy-start | bytes 6291460
  395.1 56.3 %all-to-all-start.5 = ((bf16[16,32,16,128]{3,1,2,0:T(8,128)(2,1)}), bf16[16,32,16,128]{3,1,2,0:T(8,128)(2,1)}, u32[]{:S(2)}, u32[]{:S(2)}) async-start(bf16[16,32,16,128]{3,1,2,0:T(8,128)(2,1)} %stack.41), calls=%async_computation.5 | async-start | bytes 4194304 | tf_op jit(solution)/shard_map/all_to_all | solution.py:32
  454.1 94.0 %all-to-all-start.14 = ((bf16[16,32,16,128]{3,1,2,0:T(8,128)(2,1)}), bf16[16,32,16,128]{3,1,2,0:T(8,128)(2,1)}, u32[]{:S(2)}, u32[]{:S(2)}) async-start(bf16[16,32,16,128]{3,1,2,0:T(8,128)(2,1)} %stack.50), calls=%async_computation.14 | async-start | bytes 4194304 | tf_op jit(solution)/shard_map/all_to_all | solution.py:32
  479.7 6.5 copy-start.51
  479.7 6.5 copy-start.52
  479.7 6.5 copy-start.53
  479.7 6.5 copy-start.54
  548.8 10.3 %all-to-all-start.7 = ((f32[4,128,16]{1,2,0:T(8,128)}), f32[4,128,16]{1,2,0:T(8,128)}, u32[]{:S(2)}, u32[]{:S(2)}) async-start(f32[4,128,16]{1,2,0:T(8,128)} %stack.43), calls=%async_computation.7 | async-start | bytes 65536 | tf_op jit(solution)/shard_map/all_to_all | solution.py:32
  559.7 9.6 %all-to-all-start.9 = ((f32[4,128,16]{1,2,0:T(8,128)}), f32[4,128,16]{1,2,0:T(8,128)}, u32[]{:S(2)}, u32[]{:S(2)}) async-start(f32[4,128,16]{1,2,0:T(8,128)} %stack.45), calls=%async_computation.9 | async-start | bytes 65536 | tf_op jit(solution)/shard_map/all_to_all | solution.py:32
  569.3 14.1 %all-to-all-start.11 = ((f32[8,1,1024]{2,1,0:T(1,128)}), f32[8,1,1024]{2,1,0:T(1,128)}, u32[]{:S(2)}, u32[]{:S(2)}) async-start(f32[8,1,1024]{2,1,0:T(1,128)} %reshape.1066), calls=%async_computation.11 | async-start | bytes 65536 | tf_op jit(solution)/shard_map/all_to_all | solution.py:32
  583.4 12.0 %all-to-all-start.13 = ((f32[8,1,1024]{2,1,0:T(1,128)}), f32[8,1,1024]{2,1,0:T(1,128)}, u32[]{:S(2)}, u32[]{:S(2)}) async-start(f32[8,1,1024]{2,1,0:T(1,128)} %reshape.1064), calls=%async_computation.13 | async-start | bytes 65536 | tf_op jit(solution)/shard_map/all_to_all | solution.py:32
  595.3 11.8 %all-to-all-start.15 = ((f32[16,1,512]{2,1,0:T(1,128)}), f32[16,1,512]{2,1,0:T(1,128)}, u32[]{:S(2)}, u32[]{:S(2)}) async-start(f32[16,1,512]{2,1,0:T(1,128)} %reshape.1060), calls=%async_computation.15 | async-start | bytes 65536 | tf_op jit(solution)/shard_map/all_to_all | solution.py:32
  607.1 12.6 %all-to-all-start.17 = ((f32[16,1,512]{2,1,0:T(1,128)}), f32[16,1,512]{2,1,0:T(1,128)}, u32[]{:S(2)}, u32[]{:S(2)}) async-start(f32[16,1,512]{2,1,0:T(1,128)} %reshape.1062), calls=%async_computation.17 | async-start | bytes 65536 | tf_op jit(solution)/shard_map/all_to_all | solution.py:32
  622.6 6.6 copy-start.61
  622.6 46.3 %all-to-all-start.8 = ((bf16[4,128,16,128]{1,3,2,0:T(8,128)(2,1)}), bf16[4,128,16,128]{1,3,2,0:T(8,128)(2,1)}, u32[]{:S(2)}, u32[]{:S(2)}) async-start(bf16[4,128,16,128]{1,3,2,0:T(8,128)(2,1)} %stack.44), calls=%async_computation.8 | async-start | bytes 4194304 | tf_op jit(solution)/shard_map/all_to_all | solution.py:32
  671.8 53.7 %all-to-all-start.12 = ((bf16[8,64,16,128]{3,1,2,0:T(8,128)(2,1)}), bf16[8,64,16,128]{3,1,2,0:T(8,128)(2,1)}, u32[]{:S(2)}, u32[]{:S(2)}) async-start(bf16[8,64,16,128]{3,1,2,0:T(8,128)(2,1)} %stack.48), calls=%async_computation.12 | async-start | bytes 4194304 | tf_op jit(solution)/shard_map/all_to_all | solution.py:32
  728.2 83.5 %all-to-all-start.16 = ((bf16[16,32,16,128]{3,1,2,0:T(8,128)(2,1)}), bf16[16,32,16,128]{3,1,2,0:T(8,128)(2,1)}, u32[]{:S(2)}, u32[]{:S(2)}) async-start(bf16[16,32,16,128]{3,1,2,0:T(8,128)(2,1)} %stack.52), calls=%async_computation.16 | async-start | bytes 4194304 | tf_op jit(solution)/shard_map/all_to_all | solution.py:32
  750.7 7.3 copy-start.46
  764.4 13.9 %copy-start.5 = (bf16[16,32,16,128]{3,1,0,2:T(8,128)(2,1)}, bf16[16,32,16,128]{3,1,0,2:T(8,128)(2,1)S(1)}, u32[]{:S(2)}) copy-start(bf16[16,32,16,128]{3,1,0,2:T(8,128)(2,1)S(1)} %copy.419) | copy-start | bytes 6291460
  (52 other events, 121.5 us)
